TPU v7x, 32 devices: a whole 2x2x4 slice. The times are simulated.
32 devices in a mesh: grp: 2 (over x), wide: 16 (over z, y, core).
Axes of the slice: x: 2, y: 2, z: 4, core: 2. Of those that a mesh axis runs over, the one named last changes fastest.
Arguments:
- query_maps: bfloat16 [4096, 1024], P(('grp', 'wide')), parts along dimension 0
- source_maps: bfloat16 [4096, 1024], P(('grp', 'wide')), parts along dimension 0
- hubs: int32 [8], P('grp'), parts along dimension 0, may hold values from 0 to 15, as said below
- pick: int32 [32, 2], P(('grp', 'wide')), parts along dimension 0, may hold values from 0 to 3, all different within a row
- weight_first: bfloat16 [16, 1, 3, 3, 3, 3], replicated, may hold values from -0.625 to 0.625
- bias_first: float32 [16], replicated, may hold values from -0.6 to 0.6
- weight_second: bfloat16 [1, 16, 3, 3, 3, 3], replicated, may hold values from -0.15625 to 0.15625
- bias_second: float32 [1], replicated, may hold values from 0 to 0.2
Outputs:
- consensus: float32 [32, 2, 128, 128], P(('grp', 'wide')), parts along dimension 0
There are 2 independent parts, one for each index of `grp`. A program takes and returns all parts, laid end to end along the dimension named above; an argument that names none is the same for every part. Nothing has to cross between parts.
Inputs may be any that keep to these rules, and one draw needn't show every extreme that they name: `hubs`: distinct photo indices of the batch.
All inputs are finite; a program needn't handle non-finite values.
Results may differ from a plain program's by a relative error of at most 0.0063.
Values may be sent and summed in bfloat16 or wider, within the bound.
No kernel may reach another device: no remote copies, remote signals or barrier semaphores. Data moves between devices by JAX's collectives and lax.ppermute only.
A program may use at most 64 MiB of HBM per device.

v0:
```python
import jax
import jax.numpy as jnp
from jax import lax
from jax.sharding import PartitionSpec as P

HQ = 4
WQ = 32
HUBS = 4


def spread(value, axis, source):
    kept = jnp.where(lax.axis_index(axis) == source, value, 0).astype(value.dtype)
    return lax.psum(kept, axis)


def conv_volume(volume, kernel):
    padded = jnp.pad(volume, ((1, 1), (0, 0), (0, 0), (0, 0), (0, 0)))
    height = volume.shape[0]
    result = None
    for offset in range(3):
        term = lax.conv_general_dilated(
            padded[offset : offset + height],
            kernel[:, :, offset],
            (1, 1, 1),
            [(1, 1), (1, 1), (1, 1)],
            preferred_element_type=jnp.float32,
        )
        result = term if result is None else result + term
    return result


def consensus_net(matrix, weight_first, bias_first, weight_second, bias_second):
    cells = matrix.shape[0]
    volume = matrix.reshape(HQ, WQ, HQ, WQ)[:, None]
    preact = conv_volume(volume, weight_first) + bias_first[None, :, None, None, None]
    hidden = jax.nn.relu(preact).astype(jnp.bfloat16)
    result = jax.nn.relu(
        conv_volume(hidden, weight_second) + bias_second[None, :, None, None, None]
    )
    return result.reshape(cells, cells)


def scaled_corr(query, sources):
    query_f = query.astype(jnp.float32)
    sources_f = sources.astype(jnp.float32)
    query_rms = jnp.sqrt(jnp.mean(query_f * query_f, axis=-1) + 1e-06)
    source_rms = jnp.sqrt(jnp.mean(sources_f * sources_f, axis=-1) + 1e-06)
    inner = jnp.einsum("ac,jbc->jab", query, sources, preferred_element_type=jnp.float32)
    scale = jnp.sqrt(jnp.float32(query.shape[1]))
    return (inner / (scale * query_rms[None, :, None] * source_rms[:, None, :])).astype(
        jnp.bfloat16
    )


def per_device(
    query_maps, source_maps, hubs, pick, weight_first, bias_first, weight_second, bias_second
):
    owners = pick[0]
    cells, channels = source_maps.shape
    chosen = jnp.zeros((2, cells, channels), jnp.bfloat16)
    for index in range(HUBS):
        arrived = spread(source_maps, "wide", hubs[index])
        chosen = jnp.where((owners == index)[:, None, None], arrived[None], chosen)
    correlation = scaled_corr(query_maps, chosen)
    volumes = jnp.concatenate([correlation, jnp.swapaxes(correlation, 1, 2)], axis=0)

    def filter_one(matrix):
        return consensus_net(matrix, weight_first, bias_first, weight_second, bias_second)

    filtered = lax.map(filter_one, volumes)
    return (filtered[:2] + jnp.swapaxes(filtered[2:], 1, 2))[None]


def solution(mesh):
    return jax.shard_map(
        per_device,
        mesh=mesh,
        in_specs=(
            P(("grp", "wide"), None),
            P(("grp", "wide"), None),
            P("grp"),
            P(("grp", "wide"), None),
            P(),
            P(),
            P(),
            P(),
        ),
        out_specs=P(("grp", "wide"), None, None, None),
        check_vma=False,
    )
```

profile of v0, /device:TPU:0, one launch (start us, length us, event | category | flops | bytes accessed | tf_op | source)
XLA Modules:
  0.0 569.2 jit_solution(4240992218030931366)
XLA Ops:
  14.3 95.2 %all-reduce.5.cloned.1.call-done = (bf16[128,1024]{1,0:T(8,128)(2,1)}, bf16[128,1024]{1,0:T(8,128)(2,1)}, bf16[128,1024]{1,0:T(8,128)(2,1)}, bf16[128,1024]{1,0:T(8,128)(2,1)}) async-done(((bf16[128,1024]{1,0:T(8,128)(2,1)}, bf16[128,1024]{1,0:T(8,128)(2,1)}, bf16[128,1024]{1,0:T(8,128)(2,1)}, bf16[128,1024]{1,0:T(8,128)(2,1)}), (bf16[128,1024]{1,0:T(8,128)(2,1)}, bf16[128,1024]{1,0:T(8,128)(2,1)}, ...) | async-done | bytes 1048592 | tf_op jit(solution)/shard_map/psum | solution.py:13
  113.0 448.3 %while.12 = (s32[]{:T(128)}, f32[4,128,128]{2,1,0:T(8,128)S(1)}, bf16[4,128,128]{2,1,0:T(8,128)(2,1)S(1)}, bf16[16,1,3,3,3,3]{0,5,4,3,2,1:T(4,128)(2,1)S(1)}, f3...) while((s32[]{:T(128)}, f32[4,128,128]{2,1,0:T(8,128)S(1)}, ...), condition=%wide.region_7.8_spmd, body=%wide.region_6.7_spmd.sunk | while | flops 100311040 | bytes 41547692 | solution.py:70
  114.6 6.2 %fusion.91 = f32[32,4,32,5,16]{2,4,3,1,0:T(8,128)} fusion(bf16[1,32,4,32,7]{3,0,4,2,1:T(2,128)(2,1)S(1)} %copy.115, bf16[16,1,3,3,3]{0,4,3,2,1:T(4,128)(2,1)S(1)} %get-tuple-element.216), kind=kOutput, calls=%fused_computation.45.clone.1 | convolution fusion | flops 14438400 | bytes 1368928 | tf_op jit(solution)/shard_map/while/body/eval_jaxpr/conv_general_dilated | solution.py:21
  121.5 6.1 %fusion.89 = f32[32,4,32,5,16]{2,4,3,1,0:T(8,128)} fusion(bf16[1,32,4,32,7]{3,0,4,2,1:T(2,128)(2,1)S(1)} %copy.113, bf16[16,1,3,3,3]{0,4,3,2,1:T(4,128)(2,1)S(1)} %get-tuple-element.214), kind=kOutput, calls=%fused_computation.43.clone.1 | convolution fusion | flops 14438400 | bytes 1368928 | tf_op jit(solution)/shard_map/while/body/eval_jaxpr/conv_general_dilated | solution.py:21
  128.3 9.4 %broadcast_select_fusion.6 = (bf16[32,4,32,5,16]{2,4,3,1,0:T(8,128)(2,1)}, bf16[32,4,32,5,16]{2,4,3,1,0:T(8,128)(2,1)}) fusion(pred[32,5]{0,1:T(8,128)(4,1)S(1)} %get-tuple-element.254, f32[16]{0:T(128)S(1)} %get-tuple-element.250, bf16[1,32,4,32,7]{3,0,4,2,1:T(2,128)(2,1)S(1)} %copy.111, bf16[16,1,3,3,3]{0,4,3,2,1:T(4,128)(2,1)S(1)} %get-tuple-element.213, ...), kind=kOutput, calls=%fused_computation.14.clone.1 | convolution fusion | flops 17387520 | bytes 3990592 | tf_op jit(solution)/shard_map/while/body/eval_jaxpr/conv_general_dilated | solution.py:21
  137.7 5.1 copy.116
  148.1 10.4 %copy.120 = bf16[16,32,4,32,7]{3,0,4,2,1:T(8,128)(2,1)} copy(bf16[16,32,4,32,7]{1,0,4,3,2:T(8,128)(2,1)} %bitcast.140) | data formatting | bytes 1835008 | tf_op jit(solution)/shard_map/while/body/eval_jaxpr/conv_general_dilated | solution.py:21
  158.5 4.9 copy.118
  166.0 10.6 %copy.119 = bf16[32,4,32,7,16]{2,4,3,1,0:T(8,128)(2,1)} copy(bf16[32,4,32,7,16]{0,4,3,2,1:T(8,128)(2,1)} %bitcast.139) | data formatting | bytes 1835008 | tf_op jit(solution)/shard_map/while/body/eval_jaxpr/convert_element_type | solution.py:36
  177.3 2.3 fusion.93
  179.6 10.4 %copy.117 = bf16[16,32,4,32,7]{3,0,4,2,1:T(8,128)(2,1)} copy(bf16[16,32,4,32,7]{1,0,4,3,2:T(8,128)(2,1)} %bitcast.141) | data formatting | bytes 1835008 | tf_op jit(solution)/shard_map/while/body/eval_jaxpr/conv_general_dilated | solution.py:21
  190.1 11.1 %convolution_select_fusion.3 = f32[32,4,32,5,1]{2,4,3,1,0:T(1,128)S(1)} fusion(bf16[16,32,4,32,7]{3,0,4,2,1:T(8,128)(2,1)} %copy.117, pred[32,5]{0,1:T(8,128)(4,1)S(1)} %get-tuple-element.254, bf16[1,16,3,3,3]{1,4,3,2,0:T(4,128)(2,1)S(1)} %get-tuple-element.219), kind=kOutput, calls=%fused_computation.23.clone.1 | convolution fusion | flops 14458880 | bytes 1000448 | tf_op jit(solution)/shard_map/while/body/eval_jaxpr/conv_general_dilated | solution.py:21
  201.1 8.9 %convolution_add_fusion.2 = f32[32,4,32,5,1]{2,4,3,1,0:T(1,128)S(1)} fusion(f32[32,4,32,5,1]{2,4,3,1,0:T(1,128)S(1)} %convolution_select_fusion.3, bf16[32,4,32,7,16]{2,4,3,1,0:T(8,128)(2,1)S(1)} %copy-done.2, bf16[1,16,3,3,3]{1,4,3,2,0:T(4,128)(2,1)S(1)} %get-tuple-element.223), kind=kOutput, calls=%fused_computation.18.clone.1 | convolution fusion | flops 14458880 | bytes 1082208 | tf_op jit(solution)/shard_map/while/body/eval_jaxpr/conv_general_dilated | solution.py:21
  210.1 10.0 %fusion.97 = f32[32,4,32,5,1]{2,4,3,1,0:T(1,128)S(1)} fusion(f32[32,4,32,5,1]{2,4,3,1,0:T(1,128)S(1)} %convolution_add_fusion.2, bf16[16,32,4,32,7]{3,0,4,2,1:T(8,128)(2,1)S(1)} %copy-done.1, pred[32,5]{0,1:T(8,128)(4,1)S(1)} %get-tuple-element.254, f32[]{:T(128)} %bitcast.137, bf16[1,16,3,3,3]{1,4,3,2,0:T(4,128)(2,1)S(1)} %get-tuple-element.225), kind=kOutput, calls=%fused_computation.22.clone.1 | convolution fusion | flops 14520320 | bytes 1082372 | tf_op jit(solution)/shard_map/while/body/eval_jaxpr/conv_general_dilated | solution.py:21
  226.3 6.2 %fusion.91 = f32[32,4,32,5,16]{2,4,3,1,0:T(8,128)} fusion(bf16[1,32,4,32,7]{3,0,4,2,1:T(2,128)(2,1)S(1)} %copy.115, bf16[16,1,3,3,3]{0,4,3,2,1:T(4,128)(2,1)S(1)} %get-tuple-element.216), kind=kOutput, calls=%fused_computation.45.clone.1 | convolution fusion | flops 14438400 | bytes 1368928 | tf_op jit(solution)/shard_map/while/body/eval_jaxpr/conv_general_dilated | solution.py:21
  233.2 6.1 %fusion.89 = f32[32,4,32,5,16]{2,4,3,1,0:T(8,128)} fusion(bf16[1,32,4,32,7]{3,0,4,2,1:T(2,128)(2,1)S(1)} %copy.113, bf16[16,1,3,3,3]{0,4,3,2,1:T(4,128)(2,1)S(1)} %get-tuple-element.214), kind=kOutput, calls=%fused_computation.43.clone.1 | convolution fusion | flops 14438400 | bytes 1368928 | tf_op jit(solution)/shard_map/while/body/eval_jaxpr/conv_general_dilated | solution.py:21
  240.0 9.4 %broadcast_select_fusion.6 = (bf16[32,4,32,5,16]{2,4,3,1,0:T(8,128)(2,1)}, bf16[32,4,32,5,16]{2,4,3,1,0:T(8,128)(2,1)}) fusion(pred[32,5]{0,1:T(8,128)(4,1)S(1)} %get-tuple-element.254, f32[16]{0:T(128)S(1)} %get-tuple-element.250, bf16[1,32,4,32,7]{3,0,4,2,1:T(2,128)(2,1)S(1)} %copy.111, bf16[16,1,3,3,3]{0,4,3,2,1:T(4,128)(2,1)S(1)} %get-tuple-element.213, ...), kind=kOutput, calls=%fused_computation.14.clone.1 | convolution fusion | flops 17387520 | bytes 3990592 | tf_op jit(solution)/shard_map/while/body/eval_jaxpr/conv_general_dilated | solution.py:21
  249.4 5.2 copy.116
  259.8 10.4 %copy.120 = bf16[16,32,4,32,7]{3,0,4,2,1:T(8,128)(2,1)} copy(bf16[16,32,4,32,7]{1,0,4,3,2:T(8,128)(2,1)} %bitcast.140) | data formatting | bytes 1835008 | tf_op jit(solution)/shard_map/while/body/eval_jaxpr/conv_general_dilated | solution.py:21
  270.2 4.9 copy.118
  277.7 10.6 %copy.119 = bf16[32,4,32,7,16]{2,4,3,1,0:T(8,128)(2,1)} copy(bf16[32,4,32,7,16]{0,4,3,2,1:T(8,128)(2,1)} %bitcast.139) | data formatting | bytes 1835008 | tf_op jit(solution)/shard_map/while/body/eval_jaxpr/convert_element_type | solution.py:36
  291.3 10.4 %copy.117 = bf16[16,32,4,32,7]{3,0,4,2,1:T(8,128)(2,1)} copy(bf16[16,32,4,32,7]{1,0,4,3,2:T(8,128)(2,1)} %bitcast.141) | data formatting | bytes 1835008 | tf_op jit(solution)/shard_map/while/body/eval_jaxpr/conv_general_dilated | solution.py:21
  301.8 11.2 %convolution_select_fusion.3 = f32[32,4,32,5,1]{2,4,3,1,0:T(1,128)S(1)} fusion(bf16[16,32,4,32,7]{3,0,4,2,1:T(8,128)(2,1)} %copy.117, pred[32,5]{0,1:T(8,128)(4,1)S(1)} %get-tuple-element.254, bf16[1,16,3,3,3]{1,4,3,2,0:T(4,128)(2,1)S(1)} %get-tuple-element.219), kind=kOutput, calls=%fused_computation.23.clone.1 | convolution fusion | flops 14458880 | bytes 1000448 | tf_op jit(solution)/shard_map/while/body/eval_jaxpr/conv_general_dilated | solution.py:21
  313.0 8.9 %convolution_add_fusion.2 = f32[32,4,32,5,1]{2,4,3,1,0:T(1,128)S(1)} fusion(f32[32,4,32,5,1]{2,4,3,1,0:T(1,128)S(1)} %convolution_select_fusion.3, bf16[32,4,32,7,16]{2,4,3,1,0:T(8,128)(2,1)S(1)} %copy-done.2, bf16[1,16,3,3,3]{1,4,3,2,0:T(4,128)(2,1)S(1)} %get-tuple-element.223), kind=kOutput, calls=%fused_computation.18.clone.1 | convolution fusion | flops 14458880 | bytes 1082208 | tf_op jit(solution)/shard_map/while/body/eval_jaxpr/conv_general_dilated | solution.py:21
  322.0 9.7 %fusion.97 = f32[32,4,32,5,1]{2,4,3,1,0:T(1,128)S(1)} fusion(f32[32,4,32,5,1]{2,4,3,1,0:T(1,128)S(1)} %convolution_add_fusion.2, bf16[16,32,4,32,7]{3,0,4,2,1:T(8,128)(2,1)S(1)} %copy-done.1, pred[32,5]{0,1:T(8,128)(4,1)S(1)} %get-tuple-element.254, f32[]{:T(128)} %bitcast.137, bf16[1,16,3,3,3]{1,4,3,2,0:T(4,128)(2,1)S(1)} %get-tuple-element.225), kind=kOutput, calls=%fused_computation.22.clone.1 | convolution fusion | flops 14520320 | bytes 1082372 | tf_op jit(solution)/shard_map/while/body/eval_jaxpr/conv_general_dilated | solution.py:21
  338.0 6.2 %fusion.91 = f32[32,4,32,5,16]{2,4,3,1,0:T(8,128)} fusion(bf16[1,32,4,32,7]{3,0,4,2,1:T(2,128)(2,1)S(1)} %copy.115, bf16[16,1,3,3,3]{0,4,3,2,1:T(4,128)(2,1)S(1)} %get-tuple-element.216), kind=kOutput, calls=%fused_computation.45.clone.1 | convolution fusion | flops 14438400 | bytes 1368928 | tf_op jit(solution)/shard_map/while/body/eval_jaxpr/conv_general_dilated | solution.py:21
  344.9 6.1 %fusion.89 = f32[32,4,32,5,16]{2,4,3,1,0:T(8,128)} fusion(bf16[1,32,4,32,7]{3,0,4,2,1:T(2,128)(2,1)S(1)} %copy.113, bf16[16,1,3,3,3]{0,4,3,2,1:T(4,128)(2,1)S(1)} %get-tuple-element.214), kind=kOutput, calls=%fused_computation.43.clone.1 | convolution fusion | flops 14438400 | bytes 1368928 | tf_op jit(solution)/shard_map/while/body/eval_jaxpr/conv_general_dilated | solution.py:21
  351.7 9.4 %broadcast_select_fusion.6 = (bf16[32,4,32,5,16]{2,4,3,1,0:T(8,128)(2,1)}, bf16[32,4,32,5,16]{2,4,3,1,0:T(8,128)(2,1)}) fusion(pred[32,5]{0,1:T(8,128)(4,1)S(1)} %get-tuple-element.254, f32[16]{0:T(128)S(1)} %get-tuple-element.250, bf16[1,32,4,32,7]{3,0,4,2,1:T(2,128)(2,1)S(1)} %copy.111, bf16[16,1,3,3,3]{0,4,3,2,1:T(4,128)(2,1)S(1)} %get-tuple-element.213, ...), kind=kOutput, calls=%fused_computation.14.clone.1 | convolution fusion | flops 17387520 | bytes 3990592 | tf_op jit(solution)/shard_map/while/body/eval_jaxpr/conv_general_dilated | solution.py:21
  361.1 5.3 copy.116
  371.7 10.4 %copy.120 = bf16[16,32,4,32,7]{3,0,4,2,1:T(8,128)(2,1)} copy(bf16[16,32,4,32,7]{1,0,4,3,2:T(8,128)(2,1)} %bitcast.140) | data formatting | bytes 1835008 | tf_op jit(solution)/shard_map/while/body/eval_jaxpr/conv_general_dilated | solution.py:21
  382.1 4.9 copy.118
  389.6 10.6 %copy.119 = bf16[32,4,32,7,16]{2,4,3,1,0:T(8,128)(2,1)} copy(bf16[32,4,32,7,16]{0,4,3,2,1:T(8,128)(2,1)} %bitcast.139) | data formatting | bytes 1835008 | tf_op jit(solution)/shard_map/while/body/eval_jaxpr/convert_element_type | solution.py:36
  400.9 2.3 fusion.93
  403.2 10.4 %copy.117 = bf16[16,32,4,32,7]{3,0,4,2,1:T(8,128)(2,1)} copy(bf16[16,32,4,32,7]{1,0,4,3,2:T(8,128)(2,1)} %bitcast.141) | data formatting | bytes 1835008 | tf_op jit(solution)/shard_map/while/body/eval_jaxpr/conv_general_dilated | solution.py:21
  413.7 11.0 %convolution_select_fusion.3 = f32[32,4,32,5,1]{2,4,3,1,0:T(1,128)S(1)} fusion(bf16[16,32,4,32,7]{3,0,4,2,1:T(8,128)(2,1)} %copy.117, pred[32,5]{0,1:T(8,128)(4,1)S(1)} %get-tuple-element.254, bf16[1,16,3,3,3]{1,4,3,2,0:T(4,128)(2,1)S(1)} %get-tuple-element.219), kind=kOutput, calls=%fused_computation.23.clone.1 | convolution fusion | flops 14458880 | bytes 1000448 | tf_op jit(solution)/shard_map/while/body/eval_jaxpr/conv_general_dilated | solution.py:21
  424.7 8.9 %convolution_add_fusion.2 = f32[32,4,32,5,1]{2,4,3,1,0:T(1,128)S(1)} fusion(f32[32,4,32,5,1]{2,4,3,1,0:T(1,128)S(1)} %convolution_select_fusion.3, bf16[32,4,32,7,16]{2,4,3,1,0:T(8,128)(2,1)S(1)} %copy-done.2, bf16[1,16,3,3,3]{1,4,3,2,0:T(4,128)(2,1)S(1)} %get-tuple-element.223), kind=kOutput, calls=%fused_computation.18.clone.1 | convolution fusion | flops 14458880 | bytes 1082208 | tf_op jit(solution)/shard_map/while/body/eval_jaxpr/conv_general_dilated | solution.py:21
  433.7 9.8 %fusion.97 = f32[32,4,32,5,1]{2,4,3,1,0:T(1,128)S(1)} fusion(f32[32,4,32,5,1]{2,4,3,1,0:T(1,128)S(1)} %convolution_add_fusion.2, bf16[16,32,4,32,7]{3,0,4,2,1:T(8,128)(2,1)S(1)} %copy-done.1, pred[32,5]{0,1:T(8,128)(4,1)S(1)} %get-tuple-element.254, f32[]{:T(128)} %bitcast.137, bf16[1,16,3,3,3]{1,4,3,2,0:T(4,128)(2,1)S(1)} %get-tuple-element.225), kind=kOutput, calls=%fused_computation.22.clone.1 | convolution fusion | flops 14520320 | bytes 1082372 | tf_op jit(solution)/shard_map/while/body/eval_jaxpr/conv_general_dilated | solution.py:21
  449.9 6.2 %fusion.91 = f32[32,4,32,5,16]{2,4,3,1,0:T(8,128)} fusion(bf16[1,32,4,32,7]{3,0,4,2,1:T(2,128)(2,1)S(1)} %copy.115, bf16[16,1,3,3,3]{0,4,3,2,1:T(4,128)(2,1)S(1)} %get-tuple-element.216), kind=kOutput, calls=%fused_computation.45.clone.1 | convolution fusion | flops 14438400 | bytes 1368928 | tf_op jit(solution)/shard_map/while/body/eval_jaxpr/conv_general_dilated | solution.py:21
  456.8 6.1 %fusion.89 = f32[32,4,32,5,16]{2,4,3,1,0:T(8,128)} fusion(bf16[1,32,4,32,7]{3,0,4,2,1:T(2,128)(2,1)S(1)} %copy.113, bf16[16,1,3,3,3]{0,4,3,2,1:T(4,128)(2,1)S(1)} %get-tuple-element.214), kind=kOutput, calls=%fused_computation.43.clone.1 | convolution fusion | flops 14438400 | bytes 1368928 | tf_op jit(solution)/shard_map/while/body/eval_jaxpr/conv_general_dilated | solution.py:21
  463.6 9.4 %broadcast_select_fusion.6 = (bf16[32,4,32,5,16]{2,4,3,1,0:T(8,128)(2,1)}, bf16[32,4,32,5,16]{2,4,3,1,0:T(8,128)(2,1)}) fusion(pred[32,5]{0,1:T(8,128)(4,1)S(1)} %get-tuple-element.254, f32[16]{0:T(128)S(1)} %get-tuple-element.250, bf16[1,32,4,32,7]{3,0,4,2,1:T(2,128)(2,1)S(1)} %copy.111, bf16[16,1,3,3,3]{0,4,3,2,1:T(4,128)(2,1)S(1)} %get-tuple-element.213, ...), kind=kOutput, calls=%fused_computation.14.clone.1 | convolution fusion | flops 17387520 | bytes 3990592 | tf_op jit(solution)/shard_map/while/body/eval_jaxpr/conv_general_dilated | solution.py:21
  473.0 5.1 copy.116
  483.4 10.4 %copy.120 = bf16[16,32,4,32,7]{3,0,4,2,1:T(8,128)(2,1)} copy(bf16[16,32,4,32,7]{1,0,4,3,2:T(8,128)(2,1)} %bitcast.140) | data formatting | bytes 1835008 | tf_op jit(solution)/shard_map/while/body/eval_jaxpr/conv_general_dilated | solution.py:21
  493.8 4.9 copy.118
  501.2 10.6 %copy.119 = bf16[32,4,32,7,16]{2,4,3,1,0:T(8,128)(2,1)} copy(bf16[32,4,32,7,16]{0,4,3,2,1:T(8,128)(2,1)} %bitcast.139) | data formatting | bytes 1835008 | tf_op jit(solution)/shard_map/while/body/eval_jaxpr/convert_element_type | solution.py:36
  514.9 10.4 %copy.117 = bf16[16,32,4,32,7]{3,0,4,2,1:T(8,128)(2,1)} copy(bf16[16,32,4,32,7]{1,0,4,3,2:T(8,128)(2,1)} %bitcast.141) | data formatting | bytes 1835008 | tf_op jit(solution)/shard_map/while/body/eval_jaxpr/conv_general_dilated | solution.py:21
  525.3 11.1 %convolution_select_fusion.3 = f32[32,4,32,5,1]{2,4,3,1,0:T(1,128)S(1)} fusion(bf16[16,32,4,32,7]{3,0,4,2,1:T(8,128)(2,1)} %copy.117, pred[32,5]{0,1:T(8,128)(4,1)S(1)} %get-tuple-element.254, bf16[1,16,3,3,3]{1,4,3,2,0:T(4,128)(2,1)S(1)} %get-tuple-element.219), kind=kOutput, calls=%fused_computation.23.clone.1 | convolution fusion | flops 14458880 | bytes 1000448 | tf_op jit(solution)/shard_map/while/body/eval_jaxpr/conv_general_dilated | solution.py:21
  536.4 8.9 %convolution_add_fusion.2 = f32[32,4,32,5,1]{2,4,3,1,0:T(1,128)S(1)} fusion(f32[32,4,32,5,1]{2,4,3,1,0:T(1,128)S(1)} %convolution_select_fusion.3, bf16[32,4,32,7,16]{2,4,3,1,0:T(8,128)(2,1)S(1)} %copy-done.2, bf16[1,16,3,3,3]{1,4,3,2,0:T(4,128)(2,1)S(1)} %get-tuple-element.223), kind=kOutput, calls=%fused_computation.18.clone.1 | convolution fusion | flops 14458880 | bytes 1082208 | tf_op jit(solution)/shard_map/while/body/eval_jaxpr/conv_general_dilated | solution.py:21
  545.4 10.0 %fusion.97 = f32[32,4,32,5,1]{2,4,3,1,0:T(1,128)S(1)} fusion(f32[32,4,32,5,1]{2,4,3,1,0:T(1,128)S(1)} %convolution_add_fusion.2, bf16[16,32,4,32,7]{3,0,4,2,1:T(8,128)(2,1)S(1)} %copy-done.1, pred[32,5]{0,1:T(8,128)(4,1)S(1)} %get-tuple-element.254, f32[]{:T(128)} %bitcast.137, bf16[1,16,3,3,3]{1,4,3,2,0:T(4,128)(2,1)S(1)} %get-tuple-element.225), kind=kOutput, calls=%fused_computation.22.clone.1 | convolution fusion | flops 14520320 | bytes 1082372 | tf_op jit(solution)/shard_map/while/body/eval_jaxpr/conv_general_dilated | solution.py:21
  (192 shorter events, 61.4 us)
Async XLA Ops:
  6.5 104.6 %copy-start.5 = (bf16[128,1024]{1,0:T(8,128)(2,1)S(1)}, bf16[128,1024]{1,0:T(8,128)(2,1)}, u32[]{:S(2)}) copy-start(bf16[128,1024]{1,0:T(8,128)(2,1)} %param.10) | copy-start | bytes 786436
  6.5 103.0 %all-reduce.5.cloned.1.call-start = ((), (), s32[]{:S(2)}) async-start(), calls=%async_computation | async-start | bytes 2097152 | tf_op jit(solution)/shard_map/psum | solution.py:13
  10.4 102.5 %copy-start.3 = (bf16[16,1,3,3,3,3]{0,5,4,3,2,1:T(4,128)(2,1)S(1)}, bf16[16,1,3,3,3,3]{0,5,4,3,2,1:T(4,128)(2,1)}, u32[]{:S(2)}) copy-start(bf16[16,1,3,3,3,3]{0,5,4,3,2,1:T(4,128)(2,1)} %param.14) | copy-start | bytes 7780
  10.5 102.5 %copy-start.4 = (bf16[1,16,3,3,3,3]{1,5,4,3,2,0:T(4,128)(2,1)S(1)}, bf16[1,16,3,3,3,3]{1,5,4,3,2,0:T(4,128)(2,1)}, u32[]{:S(2)}) copy-start(bf16[1,16,3,3,3,3]{1,5,4,3,2,0:T(4,128)(2,1)} %param.16) | copy-start | bytes 7780
  10.5 102.5 %copy-start.6 = (f32[16]{0:T(128)S(1)}, f32[16]{0:T(128)}, u32[]{:S(2)}) copy-start(f32[16]{0:T(128)} %param.15) | copy-start | bytes 196
  10.5 102.5 %copy-start.7 = (pred[32,5]{0,1:T(8,128)(4,1)S(1)}, pred[32,5]{0,1:T(8,128)(4,1)}, u32[]{:S(2)}) copy-start(pred[32,5]{0,1:T(8,128)(4,1)} %constant.157) | copy-start | bytes 484
  166.0 10.6 %copy-start = (bf16[16,32,4,4,32]{1,0,4,3,2:T(8,128)(2,1)S(1)}, bf16[16,32,4,4,32]{1,0,4,3,2:T(8,128)(2,1)}, u32[]{:S(2)}) copy-start(bf16[16,32,4,4,32]{1,0,4,3,2:T(8,128)(2,1)} %get-tuple-element.218) | copy-start | bytes 1572868 | tf_op jit(solution)/shard_map/while
  190.0 11.1 %copy-start.2 = (bf16[32,4,32,7,16]{2,4,3,1,0:T(8,128)(2,1)S(1)}, bf16[32,4,32,7,16]{2,4,3,1,0:T(8,128)(2,1)}, u32[]{:S(2)}) copy-start(bf16[32,4,32,7,16]{2,4,3,1,0:T(8,128)(2,1)} %copy.119) | copy-start | bytes 2752516 | tf_op jit(solution)/shard_map/while
  201.1 9.0 %copy-start.1 = (bf16[16,32,4,32,7]{3,0,4,2,1:T(8,128)(2,1)S(1)}, bf16[16,32,4,32,7]{3,0,4,2,1:T(8,128)(2,1)}, u32[]{:S(2)}) copy-start(bf16[16,32,4,32,7]{3,0,4,2,1:T(8,128)(2,1)} %copy.120) | copy-start | bytes 2752516 | tf_op jit(solution)/shard_map/while
  277.7 10.6 %copy-start = (bf16[16,32,4,4,32]{1,0,4,3,2:T(8,128)(2,1)S(1)}, bf16[16,32,4,4,32]{1,0,4,3,2:T(8,128)(2,1)}, u32[]{:S(2)}) copy-start(bf16[16,32,4,4,32]{1,0,4,3,2:T(8,128)(2,1)} %get-tuple-element.218) | copy-start | bytes 1572868 | tf_op jit(solution)/shard_map/while
  301.7 11.3 %copy-start.2 = (bf16[32,4,32,7,16]{2,4,3,1,0:T(8,128)(2,1)S(1)}, bf16[32,4,32,7,16]{2,4,3,1,0:T(8,128)(2,1)}, u32[]{:S(2)}) copy-start(bf16[32,4,32,7,16]{2,4,3,1,0:T(8,128)(2,1)} %copy.119) | copy-start | bytes 2752516 | tf_op jit(solution)/shard_map/while
  313.0 9.0 %copy-start.1 = (bf16[16,32,4,32,7]{3,0,4,2,1:T(8,128)(2,1)S(1)}, bf16[16,32,4,32,7]{3,0,4,2,1:T(8,128)(2,1)}, u32[]{:S(2)}) copy-start(bf16[16,32,4,32,7]{3,0,4,2,1:T(8,128)(2,1)} %copy.120) | copy-start | bytes 2752516 | tf_op jit(solution)/shard_map/while
  389.6 10.6 %copy-start = (bf16[16,32,4,4,32]{1,0,4,3,2:T(8,128)(2,1)S(1)}, bf16[16,32,4,4,32]{1,0,4,3,2:T(8,128)(2,1)}, u32[]{:S(2)}) copy-start(bf16[16,32,4,4,32]{1,0,4,3,2:T(8,128)(2,1)} %get-tuple-element.218) | copy-start | bytes 1572868 | tf_op jit(solution)/shard_map/while
  413.6 11.0 %copy-start.2 = (bf16[32,4,32,7,16]{2,4,3,1,0:T(8,128)(2,1)S(1)}, bf16[32,4,32,7,16]{2,4,3,1,0:T(8,128)(2,1)}, u32[]{:S(2)}) copy-start(bf16[32,4,32,7,16]{2,4,3,1,0:T(8,128)(2,1)} %copy.119) | copy-start | bytes 2752516 | tf_op jit(solution)/shard_map/while
  424.7 9.0 %copy-start.1 = (bf16[16,32,4,32,7]{3,0,4,2,1:T(8,128)(2,1)S(1)}, bf16[16,32,4,32,7]{3,0,4,2,1:T(8,128)(2,1)}, u32[]{:S(2)}) copy-start(bf16[16,32,4,32,7]{3,0,4,2,1:T(8,128)(2,1)} %copy.120) | copy-start | bytes 2752516 | tf_op jit(solution)/shard_map/while
  501.2 10.6 %copy-start = (bf16[16,32,4,4,32]{1,0,4,3,2:T(8,128)(2,1)S(1)}, bf16[16,32,4,4,32]{1,0,4,3,2:T(8,128)(2,1)}, u32[]{:S(2)}) copy-start(bf16[16,32,4,4,32]{1,0,4,3,2:T(8,128)(2,1)} %get-tuple-element.218) | copy-start | bytes 1572868 | tf_op jit(solution)/shard_map/while
  525.3 11.1 %copy-start.2 = (bf16[32,4,32,7,16]{2,4,3,1,0:T(8,128)(2,1)S(1)}, bf16[32,4,32,7,16]{2,4,3,1,0:T(8,128)(2,1)}, u32[]{:S(2)}) copy-start(bf16[32,4,32,7,16]{2,4,3,1,0:T(8,128)(2,1)} %copy.119) | copy-start | bytes 2752516 | tf_op jit(solution)/shard_map/while
  536.4 9.0 %copy-start.1 = (bf16[16,32,4,32,7]{3,0,4,2,1:T(8,128)(2,1)S(1)}, bf16[16,32,4,32,7]{3,0,4,2,1:T(8,128)(2,1)}, u32[]{:S(2)}) copy-start(bf16[16,32,4,32,7]{3,0,4,2,1:T(8,128)(2,1)} %copy.120) | copy-start | bytes 2752516 | tf_op jit(solution)/shard_map/while
Sparse Core Ops, SparseCore 0:
  12.6 96.8 all-reduce.4
where the time goes:
time: 572 us; the launch traced here: 569 us
  matrix products  208 us (36%)
  local copies, waits for them, and re-layouts  195 us (34%)
  waiting for transfers between devices  95.2 us (17%)
  other arithmetic  35.3 us (6%)
  loops' own time  19.6 us (3%)
  between operations  16.2 us (3%)
    conv_general_dilated x24, matrix products, conv_volume(): lax.conv_general_dilated(padded[offset:offset + height], kernel[:, :, off...  206 us
    psum x1, waiting for transfers between devices, spread(): return lax.psum(kept, axis)  95.2 us
    conv_general_dilated x52, local copies, waits for them, and re-layouts, conv_volume(): lax.conv_general_dilated(padded[offset:offset + height], kernel[:, :, off...  89.9 us
    convert_element_type x20, local copies, waits for them, and re-layouts, consensus_net(): hidden = jax.nn.relu(preact).astype(jnp.bfloat16)  85.1 us
    conv_general_dilated x20, other arithmetic, conv_volume(): lax.conv_general_dilated(padded[offset:offset + height], kernel[:, :, off...  19.8 us
    another operation x1, loops' own time, per_device(): filtered = lax.map(filter_one, volumes)  19.6 us
    slice x24, local copies, waits for them, and re-layouts, conv_volume(): padded[offset:offset + height]  13.8 us
  transfers between devices with their start and end apart: 1, of which 1 were waited for; matrix products, arithmetic and copies ran while one was open for 0% of the time, Pallas kernels for 0%

commit v1 on v0

--- a/solution.py
+++ b/solution.py
@@ -10,7 +10,7 @@
 
 def spread(value, axis, source):
     kept = jnp.where(lax.axis_index(axis) == source, value, 0).astype(value.dtype)
-    return lax.psum(kept, axis)
+    return jnp.sum(lax.all_gather(kept, axis), axis=0)
 
 
 def conv_volume(volume, kernel):

time: 572 us -> 685 us (1.20)
  waiting for transfers between devices: 95.2 us -> 195 us
  other arithmetic: 35.3 us -> 46.6 us
    all_gather x0 -> x4, waiting for transfers between devices: none -> 193 us  [spread(): return jnp.sum(lax.all_gather(kept, axis), axis=0)]
    psum x1 -> x0, waiting for transfers between devices: 95.2 us -> none  [spread(): return lax.psum(kept, axis)]
    reduce_sum x0 -> x4, other arithmetic: none -> 12.5 us  [spread(): return jnp.sum(lax.all_gather(kept, axis), axis=0)]
  transfers between devices with their start and end apart: 1 -> 4, of which waited for: 1 -> 4; matrix products, arithmetic and copies ran while one was open for 0% -> 2% of each run, Pallas kernels for 0% -> 0%
where the time goes in v1:
time: 685 us; the launch traced here: 679 us
  matrix products  206 us (30%)
  local copies, waits for them, and re-layouts  195 us (28%)
  waiting for transfers between devices  195 us (28%)
  other arithmetic  46.6 us (7%)
  loops' own time  19.6 us (3%)
  between operations  15.9 us (2%)
    conv_general_dilated x24, matrix products, conv_volume(): lax.conv_general_dilated(padded[offset:offset + height], kernel[:, :, off...  206 us
    all_gather x4, waiting for transfers between devices, spread(): return jnp.sum(lax.all_gather(kept, axis), axis=0)  193 us
    conv_general_dilated x52, local copies, waits for them, and re-layouts, conv_volume(): lax.conv_general_dilated(padded[offset:offset + height], kernel[:, :, off...  89.9 us
    convert_element_type x20, local copies, waits for them, and re-layouts, consensus_net(): hidden = jax.nn.relu(preact).astype(jnp.bfloat16)  84.9 us
    conv_general_dilated x20, other arithmetic, conv_volume(): lax.conv_general_dilated(padded[offset:offset + height], kernel[:, :, off...  19.8 us
    another operation x1, loops' own time, per_device(): filtered = lax.map(filter_one, volumes)  19.6 us
    slice x24, local copies, waits for them, and re-layouts, conv_volume(): padded[offset:offset + height]  13.7 us
  transfers between devices with their start and end apart: 4, of which 4 were waited for; matrix products, arithmetic and copies ran while one was open for 2% of the time, Pallas kernels for 0%

profile of v1, /device:TPU:0, one launch (start us, length us, event | category | flops | bytes accessed | tf_op | source)
XLA Modules:
  0.0 678.9 jit_solution(17999909194057483840)
XLA Ops:
  16.3 49.4 %all-gather.9.cloned.1.call-done = bf16[2048,1024]{1,0:T(8,128)(2,1)} async-done(((bf16[128,1024]{1,0:T(8,128)(2,1)}), bf16[2048,1024]{1,0:T(8,128)(2,1)}) %all-gather.9.cloned.1.call-update) | async-done | bytes 4194320 | tf_op jit(solution)/shard_map/all_gather | solution.py:13
  68.8 48.0 %all-gather.11.cloned.1.call-done = bf16[2048,1024]{1,0:T(8,128)(2,1)} async-done(((bf16[128,1024]{1,0:T(8,128)(2,1)}), bf16[2048,1024]{1,0:T(8,128)(2,1)}) %all-gather.11.cloned.1.call-update) | async-done | bytes 4194320 | tf_op jit(solution)/shard_map/all_gather | solution.py:13
  119.9 48.0 %all-gather.13.cloned.1.call-done = bf16[2048,1024]{1,0:T(8,128)(2,1)} async-done(((bf16[128,1024]{1,0:T(8,128)(2,1)}), bf16[2048,1024]{1,0:T(8,128)(2,1)}) %all-gather.13.cloned.1.call-update) | async-done | bytes 4194320 | tf_op jit(solution)/shard_map/all_gather | solution.py:13
  171.0 47.8 %all-gather.15.cloned.1.call-done = bf16[2048,1024]{1,0:T(8,128)(2,1)} async-done(((bf16[128,1024]{1,0:T(8,128)(2,1)}), bf16[2048,1024]{1,0:T(8,128)(2,1)}) %all-gather.15.cloned.1.call-update) | async-done | bytes 4194320 | tf_op jit(solution)/shard_map/all_gather | solution.py:13
  223.1 448.2 %while.12 = (s32[]{:T(128)}, f32[4,128,128]{2,1,0:T(8,128)S(1)}, bf16[4,128,128]{2,1,0:T(8,128)(2,1)S(1)}, bf16[16,1,3,3,3,3]{0,5,4,3,2,1:T(4,128)(2,1)S(1)}, f3...) while((s32[]{:T(128)}, f32[4,128,128]{2,1,0:T(8,128)S(1)}, ...), condition=%wide.region_7.8_spmd, body=%wide.region_6.7_spmd.sunk | while | flops 100311040 | bytes 41547692 | solution.py:70
  224.8 6.2 fusion.91
  231.6 6.1 fusion.89
  238.4 9.4 %broadcast_select_fusion.6 = (bf16[32,4,32,5,16]{2,4,3,1,0:T(8,128)(2,1)}, bf16[32,4,32,5,16]{2,4,3,1,0:T(8,128)(2,1)}) fusion(pred[32,5]{0,1:T(8,128)(4,1)S(1)} %get-tuple-element.250, f32[16]{0:T(128)S(1)} %get-tuple-element.246, bf16[1,32,4,32,7]{3,0,4,2,1:T(2,128)(2,1)S(1)} %copy.111, bf16[16,1,3,3,3]{0,4,3,2,1:T(4,128)(2,1)S(1)} %get-tuple-element.209, ...), kind=kOutput, calls=%fused_computation.14.clone.1 | convolution fusion | flops 17387520 | bytes 3990592 | tf_op jit(solution)/shard_map/while/body/eval_jaxpr/conv_general_dilated | solution.py:21
  247.8 5.1 copy.116
  258.2 10.4 %copy.120 = bf16[16,32,4,32,7]{3,0,4,2,1:T(8,128)(2,1)} copy(bf16[16,32,4,32,7]{1,0,4,3,2:T(8,128)(2,1)} %bitcast.144) | data formatting | bytes 1835008 | tf_op jit(solution)/shard_map/while/body/eval_jaxpr/conv_general_dilated | solution.py:21
  268.6 4.9 copy.118
  276.1 10.5 %copy.119 = bf16[32,4,32,7,16]{2,4,3,1,0:T(8,128)(2,1)} copy(bf16[32,4,32,7,16]{0,4,3,2,1:T(8,128)(2,1)} %bitcast.143) | data formatting | bytes 1835008 | tf_op jit(solution)/shard_map/while/body/eval_jaxpr/convert_element_type | solution.py:36
  289.7 10.4 %copy.117 = bf16[16,32,4,32,7]{3,0,4,2,1:T(8,128)(2,1)} copy(bf16[16,32,4,32,7]{1,0,4,3,2:T(8,128)(2,1)} %bitcast.145) | data formatting | bytes 1835008 | tf_op jit(solution)/shard_map/while/body/eval_jaxpr/conv_general_dilated | solution.py:21
  300.1 11.1 %convolution_select_fusion.3 = f32[32,4,32,5,1]{2,4,3,1,0:T(1,128)S(1)} fusion(bf16[16,32,4,32,7]{3,0,4,2,1:T(8,128)(2,1)} %copy.117, pred[32,5]{0,1:T(8,128)(4,1)S(1)} %get-tuple-element.250, bf16[1,16,3,3,3]{1,4,3,2,0:T(4,128)(2,1)S(1)} %get-tuple-element.215), kind=kOutput, calls=%fused_computation.23.clone.1 | convolution fusion | flops 14458880 | bytes 1000448 | tf_op jit(solution)/shard_map/while/body/eval_jaxpr/conv_general_dilated | solution.py:21
  311.2 8.9 %convolution_add_fusion.2 = f32[32,4,32,5,1]{2,4,3,1,0:T(1,128)S(1)} fusion(f32[32,4,32,5,1]{2,4,3,1,0:T(1,128)S(1)} %convolution_select_fusion.3, bf16[32,4,32,7,16]{2,4,3,1,0:T(8,128)(2,1)S(1)} %copy-done.2, bf16[1,16,3,3,3]{1,4,3,2,0:T(4,128)(2,1)S(1)} %get-tuple-element.219), kind=kOutput, calls=%fused_computation.18.clone.1 | convolution fusion | flops 14458880 | bytes 1082208 | tf_op jit(solution)/shard_map/while/body/eval_jaxpr/conv_general_dilated | solution.py:21
  320.2 10.0 %fusion.97 = f32[32,4,32,5,1]{2,4,3,1,0:T(1,128)S(1)} fusion(f32[32,4,32,5,1]{2,4,3,1,0:T(1,128)S(1)} %convolution_add_fusion.2, bf16[16,32,4,32,7]{3,0,4,2,1:T(8,128)(2,1)S(1)} %copy-done.1, pred[32,5]{0,1:T(8,128)(4,1)S(1)} %get-tuple-element.250, f32[]{:T(128)} %bitcast.141, bf16[1,16,3,3,3]{1,4,3,2,0:T(4,128)(2,1)S(1)} %get-tuple-element.221), kind=kOutput, calls=%fused_computation.22.clone.1 | convolution fusion | flops 14520320 | bytes 1082372 | tf_op jit(solution)/shard_map/while/body/eval_jaxpr/conv_general_dilated | solution.py:21
  336.4 6.2 fusion.91
  343.2 6.1 fusion.89
  350.1 9.4 %broadcast_select_fusion.6 = (bf16[32,4,32,5,16]{2,4,3,1,0:T(8,128)(2,1)}, bf16[32,4,32,5,16]{2,4,3,1,0:T(8,128)(2,1)}) fusion(pred[32,5]{0,1:T(8,128)(4,1)S(1)} %get-tuple-element.250, f32[16]{0:T(128)S(1)} %get-tuple-element.246, bf16[1,32,4,32,7]{3,0,4,2,1:T(2,128)(2,1)S(1)} %copy.111, bf16[16,1,3,3,3]{0,4,3,2,1:T(4,128)(2,1)S(1)} %get-tuple-element.209, ...), kind=kOutput, calls=%fused_computation.14.clone.1 | convolution fusion | flops 17387520 | bytes 3990592 | tf_op jit(solution)/shard_map/while/body/eval_jaxpr/conv_general_dilated | solution.py:21
  359.4 5.2 copy.116
  369.9 10.4 %copy.120 = bf16[16,32,4,32,7]{3,0,4,2,1:T(8,128)(2,1)} copy(bf16[16,32,4,32,7]{1,0,4,3,2:T(8,128)(2,1)} %bitcast.144) | data formatting | bytes 1835008 | tf_op jit(solution)/shard_map/while/body/eval_jaxpr/conv_general_dilated | solution.py:21
  380.3 4.9 copy.118
  387.7 10.5 %copy.119 = bf16[32,4,32,7,16]{2,4,3,1,0:T(8,128)(2,1)} copy(bf16[32,4,32,7,16]{0,4,3,2,1:T(8,128)(2,1)} %bitcast.143) | data formatting | bytes 1835008 | tf_op jit(solution)/shard_map/while/body/eval_jaxpr/convert_element_type | solution.py:36
  401.4 10.4 %copy.117 = bf16[16,32,4,32,7]{3,0,4,2,1:T(8,128)(2,1)} copy(bf16[16,32,4,32,7]{1,0,4,3,2:T(8,128)(2,1)} %bitcast.145) | data formatting | bytes 1835008 | tf_op jit(solution)/shard_map/while/body/eval_jaxpr/conv_general_dilated | solution.py:21
  411.8 11.2 %convolution_select_fusion.3 = f32[32,4,32,5,1]{2,4,3,1,0:T(1,128)S(1)} fusion(bf16[16,32,4,32,7]{3,0,4,2,1:T(8,128)(2,1)} %copy.117, pred[32,5]{0,1:T(8,128)(4,1)S(1)} %get-tuple-element.250, bf16[1,16,3,3,3]{1,4,3,2,0:T(4,128)(2,1)S(1)} %get-tuple-element.215), kind=kOutput, calls=%fused_computation.23.clone.1 | convolution fusion | flops 14458880 | bytes 1000448 | tf_op jit(solution)/shard_map/while/body/eval_jaxpr/conv_general_dilated | solution.py:21
  423.1 8.9 %convolution_add_fusion.2 = f32[32,4,32,5,1]{2,4,3,1,0:T(1,128)S(1)} fusion(f32[32,4,32,5,1]{2,4,3,1,0:T(1,128)S(1)} %convolution_select_fusion.3, bf16[32,4,32,7,16]{2,4,3,1,0:T(8,128)(2,1)S(1)} %copy-done.2, bf16[1,16,3,3,3]{1,4,3,2,0:T(4,128)(2,1)S(1)} %get-tuple-element.219), kind=kOutput, calls=%fused_computation.18.clone.1 | convolution fusion | flops 14458880 | bytes 1082208 | tf_op jit(solution)/shard_map/while/body/eval_jaxpr/conv_general_dilated | solution.py:21
  432.0 9.7 %fusion.97 = f32[32,4,32,5,1]{2,4,3,1,0:T(1,128)S(1)} fusion(f32[32,4,32,5,1]{2,4,3,1,0:T(1,128)S(1)} %convolution_add_fusion.2, bf16[16,32,4,32,7]{3,0,4,2,1:T(8,128)(2,1)S(1)} %copy-done.1, pred[32,5]{0,1:T(8,128)(4,1)S(1)} %get-tuple-element.250, f32[]{:T(128)} %bitcast.141, bf16[1,16,3,3,3]{1,4,3,2,0:T(4,128)(2,1)S(1)} %get-tuple-element.221), kind=kOutput, calls=%fused_computation.22.clone.1 | convolution fusion | flops 14520320 | bytes 1082372 | tf_op jit(solution)/shard_map/while/body/eval_jaxpr/conv_general_dilated | solution.py:21
  448.1 6.2 fusion.91
  454.9 6.1 fusion.89
  461.7 9.4 %broadcast_select_fusion.6 = (bf16[32,4,32,5,16]{2,4,3,1,0:T(8,128)(2,1)}, bf16[32,4,32,5,16]{2,4,3,1,0:T(8,128)(2,1)}) fusion(pred[32,5]{0,1:T(8,128)(4,1)S(1)} %get-tuple-element.250, f32[16]{0:T(128)S(1)} %get-tuple-element.246, bf16[1,32,4,32,7]{3,0,4,2,1:T(2,128)(2,1)S(1)} %copy.111, bf16[16,1,3,3,3]{0,4,3,2,1:T(4,128)(2,1)S(1)} %get-tuple-element.209, ...), kind=kOutput, calls=%fused_computation.14.clone.1 | convolution fusion | flops 17387520 | bytes 3990592 | tf_op jit(solution)/shard_map/while/body/eval_jaxpr/conv_general_dilated | solution.py:21
  471.1 5.3 copy.116
  481.7 10.4 %copy.120 = bf16[16,32,4,32,7]{3,0,4,2,1:T(8,128)(2,1)} copy(bf16[16,32,4,32,7]{1,0,4,3,2:T(8,128)(2,1)} %bitcast.144) | data formatting | bytes 1835008 | tf_op jit(solution)/shard_map/while/body/eval_jaxpr/conv_general_dilated | solution.py:21
  492.1 4.9 copy.118
  499.6 10.5 %copy.119 = bf16[32,4,32,7,16]{2,4,3,1,0:T(8,128)(2,1)} copy(bf16[32,4,32,7,16]{0,4,3,2,1:T(8,128)(2,1)} %bitcast.143) | data formatting | bytes 1835008 | tf_op jit(solution)/shard_map/while/body/eval_jaxpr/convert_element_type | solution.py:36
  513.2 10.4 %copy.117 = bf16[16,32,4,32,7]{3,0,4,2,1:T(8,128)(2,1)} copy(bf16[16,32,4,32,7]{1,0,4,3,2:T(8,128)(2,1)} %bitcast.145) | data formatting | bytes 1835008 | tf_op jit(solution)/shard_map/while/body/eval_jaxpr/conv_general_dilated | solution.py:21
  523.6 11.0 %convolution_select_fusion.3 = f32[32,4,32,5,1]{2,4,3,1,0:T(1,128)S(1)} fusion(bf16[16,32,4,32,7]{3,0,4,2,1:T(8,128)(2,1)} %copy.117, pred[32,5]{0,1:T(8,128)(4,1)S(1)} %get-tuple-element.250, bf16[1,16,3,3,3]{1,4,3,2,0:T(4,128)(2,1)S(1)} %get-tuple-element.215), kind=kOutput, calls=%fused_computation.23.clone.1 | convolution fusion | flops 14458880 | bytes 1000448 | tf_op jit(solution)/shard_map/while/body/eval_jaxpr/conv_general_dilated | solution.py:21
  534.7 8.9 %convolution_add_fusion.2 = f32[32,4,32,5,1]{2,4,3,1,0:T(1,128)S(1)} fusion(f32[32,4,32,5,1]{2,4,3,1,0:T(1,128)S(1)} %convolution_select_fusion.3, bf16[32,4,32,7,16]{2,4,3,1,0:T(8,128)(2,1)S(1)} %copy-done.2, bf16[1,16,3,3,3]{1,4,3,2,0:T(4,128)(2,1)S(1)} %get-tuple-element.219), kind=kOutput, calls=%fused_computation.18.clone.1 | convolution fusion | flops 14458880 | bytes 1082208 | tf_op jit(solution)/shard_map/while/body/eval_jaxpr/conv_general_dilated | solution.py:21
  543.6 9.8 %fusion.97 = f32[32,4,32,5,1]{2,4,3,1,0:T(1,128)S(1)} fusion(f32[32,4,32,5,1]{2,4,3,1,0:T(1,128)S(1)} %convolution_add_fusion.2, bf16[16,32,4,32,7]{3,0,4,2,1:T(8,128)(2,1)S(1)} %copy-done.1, pred[32,5]{0,1:T(8,128)(4,1)S(1)} %get-tuple-element.250, f32[]{:T(128)} %bitcast.141, bf16[1,16,3,3,3]{1,4,3,2,0:T(4,128)(2,1)S(1)} %get-tuple-element.221), kind=kOutput, calls=%fused_computation.22.clone.1 | convolution fusion | flops 14520320 | bytes 1082372 | tf_op jit(solution)/shard_map/while/body/eval_jaxpr/conv_general_dilated | solution.py:21
  559.9 6.2 fusion.91
  566.8 6.1 fusion.89
  573.6 9.4 %broadcast_select_fusion.6 = (bf16[32,4,32,5,16]{2,4,3,1,0:T(8,128)(2,1)}, bf16[32,4,32,5,16]{2,4,3,1,0:T(8,128)(2,1)}) fusion(pred[32,5]{0,1:T(8,128)(4,1)S(1)} %get-tuple-element.250, f32[16]{0:T(128)S(1)} %get-tuple-element.246, bf16[1,32,4,32,7]{3,0,4,2,1:T(2,128)(2,1)S(1)} %copy.111, bf16[16,1,3,3,3]{0,4,3,2,1:T(4,128)(2,1)S(1)} %get-tuple-element.209, ...), kind=kOutput, calls=%fused_computation.14.clone.1 | convolution fusion | flops 17387520 | bytes 3990592 | tf_op jit(solution)/shard_map/while/body/eval_jaxpr/conv_general_dilated | solution.py:21
  582.9 5.1 copy.116
  593.3 10.4 %copy.120 = bf16[16,32,4,32,7]{3,0,4,2,1:T(8,128)(2,1)} copy(bf16[16,32,4,32,7]{1,0,4,3,2:T(8,128)(2,1)} %bitcast.144) | data formatting | bytes 1835008 | tf_op jit(solution)/shard_map/while/body/eval_jaxpr/conv_general_dilated | solution.py:21
  611.2 10.5 %copy.119 = bf16[32,4,32,7,16]{2,4,3,1,0:T(8,128)(2,1)} copy(bf16[32,4,32,7,16]{0,4,3,2,1:T(8,128)(2,1)} %bitcast.143) | data formatting | bytes 1835008 | tf_op jit(solution)/shard_map/while/body/eval_jaxpr/convert_element_type | solution.py:36
  624.8 10.4 %copy.117 = bf16[16,32,4,32,7]{3,0,4,2,1:T(8,128)(2,1)} copy(bf16[16,32,4,32,7]{1,0,4,3,2:T(8,128)(2,1)} %bitcast.145) | data formatting | bytes 1835008 | tf_op jit(solution)/shard_map/while/body/eval_jaxpr/conv_general_dilated | solution.py:21
  635.3 11.1 %convolution_select_fusion.3 = f32[32,4,32,5,1]{2,4,3,1,0:T(1,128)S(1)} fusion(bf16[16,32,4,32,7]{3,0,4,2,1:T(8,128)(2,1)} %copy.117, pred[32,5]{0,1:T(8,128)(4,1)S(1)} %get-tuple-element.250, bf16[1,16,3,3,3]{1,4,3,2,0:T(4,128)(2,1)S(1)} %get-tuple-element.215), kind=kOutput, calls=%fused_computation.23.clone.1 | convolution fusion | flops 14458880 | bytes 1000448 | tf_op jit(solution)/shard_map/while/body/eval_jaxpr/conv_general_dilated | solution.py:21
  646.3 8.9 %convolution_add_fusion.2 = f32[32,4,32,5,1]{2,4,3,1,0:T(1,128)S(1)} fusion(f32[32,4,32,5,1]{2,4,3,1,0:T(1,128)S(1)} %convolution_select_fusion.3, bf16[32,4,32,7,16]{2,4,3,1,0:T(8,128)(2,1)S(1)} %copy-done.2, bf16[1,16,3,3,3]{1,4,3,2,0:T(4,128)(2,1)S(1)} %get-tuple-element.219), kind=kOutput, calls=%fused_computation.18.clone.1 | convolution fusion | flops 14458880 | bytes 1082208 | tf_op jit(solution)/shard_map/while/body/eval_jaxpr/conv_general_dilated | solution.py:21
  655.3 10.0 %fusion.97 = f32[32,4,32,5,1]{2,4,3,1,0:T(1,128)S(1)} fusion(f32[32,4,32,5,1]{2,4,3,1,0:T(1,128)S(1)} %convolution_add_fusion.2, bf16[16,32,4,32,7]{3,0,4,2,1:T(8,128)(2,1)S(1)} %copy-done.1, pred[32,5]{0,1:T(8,128)(4,1)S(1)} %get-tuple-element.250, f32[]{:T(128)} %bitcast.141, bf16[1,16,3,3,3]{1,4,3,2,0:T(4,128)(2,1)S(1)} %get-tuple-element.221), kind=kOutput, calls=%fused_computation.22.clone.1 | convolution fusion | flops 14520320 | bytes 1082372 | tf_op jit(solution)/shard_map/while/body/eval_jaxpr/conv_general_dilated | solution.py:21
  (205 shorter events, 83.1 us)
Async XLA Ops:
  6.5 59.1 %all-gather.9.cloned.1.call-start = ((), (), s32[]{:S(2)}) async-start(), calls=%async_computation | async-start | bytes 4456448 | tf_op jit(solution)/shard_map/all_gather | solution.py:13
  12.4 104.4 %all-gather.11.cloned.1.call-start = ((), (), s32[]{:S(2)}) async-start(), calls=%async_computation.1 | async-start | bytes 4456448 | tf_op jit(solution)/shard_map/all_gather | solution.py:13
  13.2 154.7 %all-gather.13.cloned.1.call-start = ((), (), s32[]{:S(2)}) async-start(), calls=%async_computation.2 | async-start | bytes 4456448 | tf_op jit(solution)/shard_map/all_gather | solution.py:13
  13.9 204.9 %all-gather.15.cloned.1.call-start = ((), (), s32[]{:S(2)}) async-start(), calls=%async_computation.3 | async-start | bytes 4456448 | tf_op jit(solution)/shard_map/all_gather | solution.py:13
  171.0 51.4 %copy-start.5 = (bf16[128,1024]{1,0:T(8,128)(2,1)S(1)}, bf16[128,1024]{1,0:T(8,128)(2,1)}, u32[]{:S(2)}) copy-start(bf16[128,1024]{1,0:T(8,128)(2,1)} %param.10) | copy-start | bytes 786436
  218.8 4.3 copy-start.3
  218.8 4.3 copy-start.4
  218.9 4.3 copy-start.6
  218.9 4.3 copy-start.7
  276.1 10.5 %copy-start = (bf16[16,32,4,4,32]{1,0,4,3,2:T(8,128)(2,1)S(1)}, bf16[16,32,4,4,32]{1,0,4,3,2:T(8,128)(2,1)}, u32[]{:S(2)}) copy-start(bf16[16,32,4,4,32]{1,0,4,3,2:T(8,128)(2,1)} %get-tuple-element.214) | copy-start | bytes 1572868 | tf_op jit(solution)/shard_map/while
  300.1 11.1 %copy-start.2 = (bf16[32,4,32,7,16]{2,4,3,1,0:T(8,128)(2,1)S(1)}, bf16[32,4,32,7,16]{2,4,3,1,0:T(8,128)(2,1)}, u32[]{:S(2)}) copy-start(bf16[32,4,32,7,16]{2,4,3,1,0:T(8,128)(2,1)} %copy.119) | copy-start | bytes 2752516 | tf_op jit(solution)/shard_map/while
  311.2 9.0 %copy-start.1 = (bf16[16,32,4,32,7]{3,0,4,2,1:T(8,128)(2,1)S(1)}, bf16[16,32,4,32,7]{3,0,4,2,1:T(8,128)(2,1)}, u32[]{:S(2)}) copy-start(bf16[16,32,4,32,7]{3,0,4,2,1:T(8,128)(2,1)} %copy.120) | copy-start | bytes 2752516 | tf_op jit(solution)/shard_map/while
  387.7 10.5 %copy-start = (bf16[16,32,4,4,32]{1,0,4,3,2:T(8,128)(2,1)S(1)}, bf16[16,32,4,4,32]{1,0,4,3,2:T(8,128)(2,1)}, u32[]{:S(2)}) copy-start(bf16[16,32,4,4,32]{1,0,4,3,2:T(8,128)(2,1)} %get-tuple-element.214) | copy-start | bytes 1572868 | tf_op jit(solution)/shard_map/while
  411.8 11.3 %copy-start.2 = (bf16[32,4,32,7,16]{2,4,3,1,0:T(8,128)(2,1)S(1)}, bf16[32,4,32,7,16]{2,4,3,1,0:T(8,128)(2,1)}, u32[]{:S(2)}) copy-start(bf16[32,4,32,7,16]{2,4,3,1,0:T(8,128)(2,1)} %copy.119) | copy-start | bytes 2752516 | tf_op jit(solution)/shard_map/while
  423.1 9.0 %copy-start.1 = (bf16[16,32,4,32,7]{3,0,4,2,1:T(8,128)(2,1)S(1)}, bf16[16,32,4,32,7]{3,0,4,2,1:T(8,128)(2,1)}, u32[]{:S(2)}) copy-start(bf16[16,32,4,32,7]{3,0,4,2,1:T(8,128)(2,1)} %copy.120) | copy-start | bytes 2752516 | tf_op jit(solution)/shard_map/while
  499.6 10.5 %copy-start = (bf16[16,32,4,4,32]{1,0,4,3,2:T(8,128)(2,1)S(1)}, bf16[16,32,4,4,32]{1,0,4,3,2:T(8,128)(2,1)}, u32[]{:S(2)}) copy-start(bf16[16,32,4,4,32]{1,0,4,3,2:T(8,128)(2,1)} %get-tuple-element.214) | copy-start | bytes 1572868 | tf_op jit(solution)/shard_map/while
  523.6 11.0 %copy-start.2 = (bf16[32,4,32,7,16]{2,4,3,1,0:T(8,128)(2,1)S(1)}, bf16[32,4,32,7,16]{2,4,3,1,0:T(8,128)(2,1)}, u32[]{:S(2)}) copy-start(bf16[32,4,32,7,16]{2,4,3,1,0:T(8,128)(2,1)} %copy.119) | copy-start | bytes 2752516 | tf_op jit(solution)/shard_map/while
  534.7 9.0 %copy-start.1 = (bf16[16,32,4,32,7]{3,0,4,2,1:T(8,128)(2,1)S(1)}, bf16[16,32,4,32,7]{3,0,4,2,1:T(8,128)(2,1)}, u32[]{:S(2)}) copy-start(bf16[16,32,4,32,7]{3,0,4,2,1:T(8,128)(2,1)} %copy.120) | copy-start | bytes 2752516 | tf_op jit(solution)/shard_map/while
  611.2 10.5 %copy-start = (bf16[16,32,4,4,32]{1,0,4,3,2:T(8,128)(2,1)S(1)}, bf16[16,32,4,4,32]{1,0,4,3,2:T(8,128)(2,1)}, u32[]{:S(2)}) copy-start(bf16[16,32,4,4,32]{1,0,4,3,2:T(8,128)(2,1)} %get-tuple-element.214) | copy-start | bytes 1572868 | tf_op jit(solution)/shard_map/while
  635.3 11.1 %copy-start.2 = (bf16[32,4,32,7,16]{2,4,3,1,0:T(8,128)(2,1)S(1)}, bf16[32,4,32,7,16]{2,4,3,1,0:T(8,128)(2,1)}, u32[]{:S(2)}) copy-start(bf16[32,4,32,7,16]{2,4,3,1,0:T(8,128)(2,1)} %copy.119) | copy-start | bytes 2752516 | tf_op jit(solution)/shard_map/while
  646.3 9.0 %copy-start.1 = (bf16[16,32,4,32,7]{3,0,4,2,1:T(8,128)(2,1)S(1)}, bf16[16,32,4,32,7]{3,0,4,2,1:T(8,128)(2,1)}, u32[]{:S(2)}) copy-start(bf16[16,32,4,32,7]{3,0,4,2,1:T(8,128)(2,1)} %copy.120) | copy-start | bytes 2752516 | tf_op jit(solution)/shard_map/while
Sparse Core Ops, SparseCore 0:
  12.6 53.0 all-gather.8
  67.8 48.8 all-gather.10
  119.0 48.8 all-gather.12
  169.9 48.8 all-gather.14
